TPU v7x, 128 devices: a whole 4x4x4 slice. The times are simulated.
128 devices in a mesh: row: 8 (over z_lo, y), col: 16 (over x, z_hi, core).
Axes of the slice: x: 4, y: 4, z: 4 (z_hi: 2, z_lo: 2; z = z_hi * 2 + z_lo), core: 2. Of those that a mesh axis runs over, the one named last changes fastest.
Arguments:
- factors: bfloat16 [10240, 3, 2048], P(('row', 'col')), may hold values from -0.59765625 to 0.59765625
- occ_energy: float32 [300], replicated, may hold values from -3 to -0.5
- vir_energy: float32 [2048], replicated, may hold values from 0.3 to 4
- slab_orbitals: int32 [3], replicated, may hold values from 0 to 299
- pair_list: int32 [16, 2], replicated, may hold values from 0 to 2
- pair_state: int32 [16], replicated, may hold values from 0 to 3
- state_shift: float32 [4], replicated, may hold values from 0.1 to 1
Outputs:
- amplitudes: float32 [16, 2048, 2048], P(None, 'row', 'col')
All inputs are finite; a program needn't handle non-finite values.
Results may differ from a plain program's by a relative error of at most 0.0003.
Values may be sent and summed in bfloat16 or wider, within the bound.
No kernel may reach another device: no remote copies, remote signals or barrier semaphores. Data moves between devices by JAX's collectives and lax.ppermute only.
A program may use at most 192 MiB of HBM per device.

v0:
```python
import jax
import jax.numpy as jnp
from jax import lax
from jax.sharding import Mesh, PartitionSpec as P


def row_ring(n_row):
    half = n_row // 2
    return list(range(half)) + [half + y for y in reversed(range(half))]


def ring_gather(shard, axis, ring):
    n = len(ring)
    position = [0] * n
    for k, r in enumerate(ring):
        position[r] = k
    right = [(ring[k], ring[(k + 1) % n]) for k in range(n)]
    left = [(ring[k], ring[(k - 1) % n]) for k in range(n)]
    ring_arr = jnp.array(ring, dtype=jnp.int32)
    me = lax.axis_index(axis)
    my_pos = jnp.array(position, dtype=jnp.int32)[me]
    out = jnp.zeros((n,) + shard.shape, shard.dtype)
    out = lax.dynamic_update_index_in_dim(out, shard, me, 0)
    go_right = go_left = shard
    n_right = n // 2
    n_left = n - 1 - n_right
    for step in range(1, n_right + 1):
        go_right = lax.ppermute(go_right, axis, right)
        out = lax.dynamic_update_index_in_dim(out, go_right, ring_arr[(my_pos - step) % n], 0)
        if step <= n_left:
            go_left = lax.ppermute(go_left, axis, left)
            out = lax.dynamic_update_index_in_dim(out, go_left, ring_arr[(my_pos + step) % n], 0)
    return out


def shards(factors, occ_energy, vir_energy, slab_orbitals, pair_list, pair_state, state_shift):
    n_row = lax.axis_size("row")
    n_colx = lax.axis_size("colx")
    n_core = lax.axis_size("core")
    n_col = n_colx * n_core
    local_aux, nocc, nvir = factors.shape
    rows_a = nvir // n_row
    cols_b = nvir // n_col
    spread_a = lax.all_to_all(
        factors.reshape(local_aux, nocc, n_row, rows_a),
        "row",
        split_axis=2,
        concat_axis=0,
        tiled=True,
    ).reshape(n_row * local_aux, nocc, rows_a)
    half_a = lax.all_gather(spread_a, "colx", axis=0, tiled=True)
    other_a = lax.ppermute(half_a, "core", [(k, (k + 1) % n_core) for k in range(n_core)])
    spread_b = lax.all_to_all(
        factors.reshape(local_aux, nocc, n_col, cols_b),
        ("colx", "core"),
        split_axis=2,
        concat_axis=0,
        tiled=True,
    ).reshape(n_col * local_aux, nocc, cols_b)
    block_b = ring_gather(spread_b, "row", row_ring(n_row))
    block_b = block_b.reshape(n_row, n_colx, n_core, local_aux, nocc, cols_b)
    me_core = lax.axis_index("core")
    contract = "xrpia,rxpjb->ijab"
    gram = jnp.einsum(
        contract,
        half_a.reshape(n_colx, n_row, local_aux, nocc, rows_a),
        lax.dynamic_index_in_dim(block_b, me_core, 2, keepdims=False),
        preferred_element_type=jnp.float32,
    ) + jnp.einsum(
        contract,
        other_a.reshape(n_colx, n_row, local_aux, nocc, rows_a),
        lax.dynamic_index_in_dim(block_b, (me_core + n_core - 1) % n_core, 2, keepdims=False),
        preferred_element_type=jnp.float32,
    )
    gram = gram.reshape(nocc * nocc, rows_a, cols_b)
    first = pair_list[:, 0]
    second = pair_list[:, 1]
    kernel = jnp.take(gram, first * nocc + second, axis=0)
    vir_a = lax.dynamic_slice_in_dim(vir_energy, lax.axis_index("row") * rows_a, rows_a)
    col_index = lax.axis_index("colx") * n_core + me_core
    vir_b = lax.dynamic_slice_in_dim(vir_energy, col_index * cols_b, cols_b)
    e_first = occ_energy[slab_orbitals[first]]
    e_second = occ_energy[slab_orbitals[second]]
    shift = state_shift[pair_state]
    denom = (
        vir_a[None, :, None]
        + vir_b[None, None, :]
        - e_first[:, None, None]
        - e_second[:, None, None]
        + shift[:, None, None]
    )
    return -kernel / denom


def solution(mesh):
    n_row, n_col = mesh.devices.shape
    sub = Mesh(mesh.devices.reshape(n_row, n_col // 2, 2), ("row", "colx", "core"))
    placed = (P(("row", "colx", "core"), None, None), P(), P(), P(), P(), P(), P())
    return jax.shard_map(
        shards,
        mesh=sub,
        in_specs=placed,
        out_specs=P(None, "row", ("colx", "core")),
        check_vma=False,
    )
```

profile of v0, /device:TPU:0, one launch (start us, length us, event | category | flops | bytes accessed | tf_op | source)
XLA Modules:
  0.0 275.2 jit_solution(11836928373755230479)
XLA Ops:
  6.5 1.4 copy.72
  7.9 20.7 %all_to_all.30 = bf16[80,3,8,256]{3,0,1,2:T(8,128)(2,1)S(1)} all-to-all(bf16[80,3,8,256]{3,0,1,2:T(8,128)(2,1)S(1)} %bitcast.118), channel_id=1, replica_groups=mesh['row'=8,'colx'=8,'core'=2] {'row'}, dimensions={2} | all-to-all | bytes 1966080 | tf_op jit(solution)/shard_map/all_to_all | solution.py:44
  28.6 1.0 copy.27
  29.7 103.7 %all-gather.2.cloned.1.call-done = bf16[5120,3,256]{2,0,1:T(8,128)(2,1)} async-done(((bf16[640,3,256]{2,0,1:T(8,128)(2,1)}), bf16[5120,3,256]{2,0,1:T(8,128)(2,1)}) %all-gather.2.cloned.1.call-update) | async-done | bytes 7864336 | tf_op jit(solution)/shard_map/all_gather | solution.py:51
  133.4 1.1 copy_bitcast_fusion.1
  134.5 3.6 %all-to-all-start = ((bf16[80,3,16,128]{3,0,1,2:T(8,128)(2,1)}), bf16[80,3,16,128]{3,0,1,2:T(8,128)(2,1)S(1)}, u32[]{:S(2)}, u32[]{:S(2)}) async-start(bf16[80,3,16,128]{3,0,1,2:T(8,128)(2,1)} %copy_bitcast_fusion.1), calls=%async_computation | async-start | bytes 1966080 | tf_op jit(solution)/shard_map/all_to_all | solution.py:53
  138.2 0.7 fusion.32
  138.9 1.9 fusion.30
  140.8 14.6 %all-to-all-done = bf16[80,3,16,128]{3,0,1,2:T(8,128)(2,1)S(1)} async-done(((bf16[80,3,16,128]{3,0,1,2:T(8,128)(2,1)}), bf16[80,3,16,128]{3,0,1,2:T(8,128)(2,1)S(1)}, u32[]{:S(2)}, u32[]{:S(2)}) %all-to-all-start) | async-done | bytes 983072 | tf_op jit(solution)/shard_map/all_to_all | solution.py:53
  155.5 1.6 collective-permute-start
  157.0 0.5 collective-permute-start.1
  157.6 0.6 dynamic_slice.37
  162.8 0.7 fusion.33
  172.5 0.8 dynamic_slice.48
  173.3 0.8 dynamic_slice.47
  174.0 0.7 gather_fusion.1
  174.7 0.7 gather_fusion.2
  179.9 0.7 gather_fusion.3
  180.6 1.7 broadcast_in_dim.51
  182.5 1.6 collective-permute-start.2
  184.0 0.5 collective-permute-start.3
  184.9 20.2 %collective-permute-done.2 = bf16[1280,3,128]{2,0,1:T(8,128)(2,1)S(1)} collective-permute-done((bf16[1280,3,128]{2,0,1:T(8,128)(2,1)S(1)}, bf16[1280,3,128]{2,0,1:T(8,128)(2,1)S(1)}, u32[]{:S(2)}, u32[]{:S(2)}) %collective-permute-start.2) | collective-permute-done | bytes 983072 | tf_op jit(solution)/shard_map/ppermute | solution.py:28
  205.0 1.5 collective-permute-start.4
  206.5 0.5 collective-permute-start.5
  207.3 19.6 %collective-permute-done.4 = bf16[1280,3,128]{2,0,1:T(8,128)(2,1)S(1)} collective-permute-done((bf16[1280,3,128]{2,0,1:T(8,128)(2,1)S(1)}, bf16[1280,3,128]{2,0,1:T(8,128)(2,1)S(1)}, u32[]{:S(2)}, u32[]{:S(2)}) %collective-permute-start.4) | collective-permute-done | bytes 983072 | tf_op jit(solution)/shard_map/ppermute | solution.py:28
  226.9 1.5 collective-permute-start.6
  228.7 19.0 %collective-permute-done.6 = bf16[1280,3,128]{2,0,1:T(8,128)(2,1)S(1)} collective-permute-done((bf16[1280,3,128]{2,0,1:T(8,128)(2,1)S(1)}, bf16[1280,3,128]{2,0,1:T(8,128)(2,1)S(1)}, u32[]{:S(2)}, u32[]{:S(2)}) %collective-permute-start.6) | collective-permute-done | bytes 983072 | tf_op jit(solution)/shard_map/ppermute | solution.py:28
  247.8 3.2 %constant_dynamic-slice_fusion.1 = (bf16[8,8,1,80,3,128]{5,3,2,1,4,0:T(8,128)(2,1)S(1)}, bf16[8,8,1,80,3,128]{5,3,2,1,4,0:T(8,128)(2,1)}) fusion(bf16[8,8,2,80,3,128]{5,3,2,1,4,0:T(8,128)(2,1)S(1)} %bitcast.111, s32[]{:T(128)S(6)} %select_n.160, s32[]{:T(128)S(6)} %select_n.162), kind=kLoop, calls=%fused_computation.40 | loop fusion | bytes 15728648 | tf_op jit(solution)/shard_map/jit(dynamic_index_in_dim)/dynamic_slice | solution.py:67
  251.1 7.7 %fusion.15 = f32[3,128,3,256]{3,1,2,0:T(8,128)S(1)} fusion(bf16[8,8,80,3,256]{4,2,1,0,3:T(8,128)(2,1)} %bitcast.42, bf16[8,8,1,80,3,128]{5,3,2,1,4,0:T(8,128)(2,1)} %get-tuple-element.8), kind=kOutput, calls=%fused_computation.16 | convolution fusion | flops 3019898880 | bytes 12976128 | tf_op jit(solution)/shard_map/xrpia,rxpjb->ijab/dot_general | solution.py:69
  258.8 6.5 %fusion.25 = f32[3,3,256,128]{2,3,0,1:T(8,128)S(1)} fusion(f32[3,128,3,256]{3,1,2,0:T(8,128)S(1)} %fusion.15, bf16[8,8,80,3,256]{4,2,1,0,3:T(8,128)(2,1)} %bitcast.120, bf16[8,8,1,80,3,128]{5,3,2,1,4,0:T(8,128)(2,1)S(1)} %get-tuple-element.7), kind=kOutput, calls=%fused_computation.18 | convolution fusion | flops 3020193792 | bytes 14155776 | tf_op jit(solution)/shard_map/xrpia,rxpjb->ijab/dot_general | solution.py:64
  265.7 0.7 gather_fusion
  266.4 1.9 add_divide_fusion
  (38 shorter events, 1.7 us)
Async XLA Ops:
  6.5 167.5 %copy-start = (f32[300]{0:T(512)S(1)}, f32[300]{0:T(512)}, u32[]{:S(2)}) copy-start(f32[300]{0:T(512)} %param.10) | copy-start | bytes 3604
  6.5 126.9 %copy-start.2 = (bf16[80,3,2048]{2,0,1:T(8,128)(2,1)S(1)}, bf16[80,3,2048]{2,0,1:T(8,128)(2,1)}, u32[]{:S(2)}) copy-start(bf16[80,3,2048]{2,0,1:T(8,128)(2,1)} %param.9) | copy-start | bytes 2949124
  6.5 126.9 %all-gather.2.cloned.1.call-start = ((), (), s32[]{:S(2)}) async-start(), calls=%async_computation.2 | async-start | bytes 8847360 | tf_op jit(solution)/shard_map/all_gather | solution.py:51
  28.6 109.6 %copy-start.4 = (s32[3]{0:T(128)S(1)}, s32[3]{0:T(128)}, u32[]{:S(2)}) copy-start(s32[3]{0:T(128)} %param.12) | copy-start | bytes 40
  28.6 110.2 %copy-start.6 = (s32[16]{0:T(128)S(1)}, s32[16]{0:T(128)}, u32[]{:S(2)}) copy-start(s32[16]{0:T(128)} %param.14) | copy-start | bytes 196
  28.6 110.2 %copy-start.5 = (s32[16,2]{0,1:T(2,128)S(1)}, s32[16,2]{0,1:T(2,128)}, u32[]{:S(2)}) copy-start(s32[16,2]{0,1:T(2,128)} %param.13) | copy-start | bytes 388
  29.7 127.9 %copy-start.3 = (s32[8]{0:T(128)S(1)}, s32[8]{0:T(128)}, u32[]{:S(2)}) copy-start(s32[8]{0:T(128)} %constant.138.clone) | copy-start | bytes 100
  29.7 150.2 %copy-start.1 = (f32[4]{0:T(128)S(1)}, f32[4]{0:T(128)}, u32[]{:S(2)}) copy-start(f32[4]{0:T(128)} %param.15) | copy-start | bytes 52
  133.4 117.6 %collective-permute-start.7 = (bf16[5120,3,256]{2,0,1:T(8,128)(2,1)}, bf16[5120,3,256]{2,0,1:T(8,128)(2,1)}, u32[]{:S(2)}, u32[]{:S(2)}) collective-permute-start(bf16[5120,3,256]{2,0,1:T(8,128)(2,1)} %all-gather.2.cloned.1.call-done), channel_id=1, source_target_pairs={{0,1},{1,0},{2,3},{3,2},{4,5},{5,4},{6,7},{7,6},{8,9},{9,8},{10,11... | collective-permute-start | bytes 23592968 | tf_op jit(solution)/shard_map/ppermute | solution.py:52
  134.5 20.9 %all-to-all-start = ((bf16[80,3,16,128]{3,0,1,2:T(8,128)(2,1)}), bf16[80,3,16,128]{3,0,1,2:T(8,128)(2,1)S(1)}, u32[]{:S(2)}, u32[]{:S(2)}) async-start(bf16[80,3,16,128]{3,0,1,2:T(8,128)(2,1)} %copy_bitcast_fusion.1), calls=%async_computation | async-start | bytes 1966080 | tf_op jit(solution)/shard_map/all_to_all | solution.py:53
  155.5 27.0 %collective-permute-start = (bf16[1280,3,128]{2,0,1:T(8,128)(2,1)S(1)}, bf16[1280,3,128]{2,0,1:T(8,128)(2,1)S(1)}, u32[]{:S(2)}, u32[]{:S(2)}) collective-permute-start(bf16[1280,3,128]{2,0,1:T(8,128)(2,1)S(1)} %bitcast.114), channel_id=1, source_target_pairs={{0,16},{16,32},{32,48},{48,112},{112,96},{96,80},{80,64},{64,0},{1... | collective-permute-start | bytes 2949128 | tf_op jit(solution)/shard_map/ppermute | solution.py:28
  157.0 27.0 %collective-permute-start.1 = (bf16[1280,3,128]{2,0,1:T(8,128)(2,1)S(1)}, bf16[1280,3,128]{2,0,1:T(8,128)(2,1)S(1)}, u32[]{:S(2)}, u32[]{:S(2)}) collective-permute-start(bf16[1280,3,128]{2,0,1:T(8,128)(2,1)S(1)} %bitcast.115), channel_id=1, source_target_pairs={{0,64},{16,0},{32,16},{48,32},{112,48},{96,112},{80,96},{64,80},{1... | collective-permute-start | bytes 2949128 | tf_op jit(solution)/shard_map/ppermute | solution.py:31
  182.5 22.5 %collective-permute-start.2 = (bf16[1280,3,128]{2,0,1:T(8,128)(2,1)S(1)}, bf16[1280,3,128]{2,0,1:T(8,128)(2,1)S(1)}, u32[]{:S(2)}, u32[]{:S(2)}) collective-permute-start(bf16[1280,3,128]{2,0,1:T(8,128)(2,1)S(1)} %collective-permute-done), channel_id=1, source_target_pairs={{0,16},{16,32},{32,48},{48,112},{112,96},{96,80},{80,64},{64,0},{1... | collective-permute-start | bytes 2949128 | tf_op jit(solution)/shard_map/ppermute | solution.py:28
  184.0 22.5 %collective-permute-start.3 = (bf16[1280,3,128]{2,0,1:T(8,128)(2,1)S(1)}, bf16[1280,3,128]{2,0,1:T(8,128)(2,1)S(1)}, u32[]{:S(2)}, u32[]{:S(2)}) collective-permute-start(bf16[1280,3,128]{2,0,1:T(8,128)(2,1)S(1)} %collective-permute-done.1), channel_id=1, source_target_pairs={{0,64},{16,0},{32,16},{48,32},{112,48},{96,112},{80,96},{64,80},{1... | collective-permute-start | bytes 2949128 | tf_op jit(solution)/shard_map/ppermute | solution.py:31
  205.0 21.9 %collective-permute-start.4 = (bf16[1280,3,128]{2,0,1:T(8,128)(2,1)S(1)}, bf16[1280,3,128]{2,0,1:T(8,128)(2,1)S(1)}, u32[]{:S(2)}, u32[]{:S(2)}) collective-permute-start(bf16[1280,3,128]{2,0,1:T(8,128)(2,1)S(1)} %collective-permute-done.2), channel_id=1, source_target_pairs={{0,16},{16,32},{32,48},{48,112},{112,96},{96,80},{80,64},{64,0},{1... | collective-permute-start | bytes 2949128 | tf_op jit(solution)/shard_map/ppermute | solution.py:28
  206.5 22.1 %collective-permute-start.5 = (bf16[1280,3,128]{2,0,1:T(8,128)(2,1)S(1)}, bf16[1280,3,128]{2,0,1:T(8,128)(2,1)S(1)}, u32[]{:S(2)}, u32[]{:S(2)}) collective-permute-start(bf16[1280,3,128]{2,0,1:T(8,128)(2,1)S(1)} %collective-permute-done.3), channel_id=1, source_target_pairs={{0,64},{16,0},{32,16},{48,32},{112,48},{96,112},{80,96},{64,80},{1... | collective-permute-start | bytes 2949128 | tf_op jit(solution)/shard_map/ppermute | solution.py:31
  226.9 20.8 %collective-permute-start.6 = (bf16[1280,3,128]{2,0,1:T(8,128)(2,1)S(1)}, bf16[1280,3,128]{2,0,1:T(8,128)(2,1)S(1)}, u32[]{:S(2)}, u32[]{:S(2)}) collective-permute-start(bf16[1280,3,128]{2,0,1:T(8,128)(2,1)S(1)} %collective-permute-done.4), channel_id=1, source_target_pairs={{0,16},{16,32},{32,48},{48,112},{112,96},{96,80},{80,64},{64,0},{1... | collective-permute-start | bytes 2949128 | tf_op jit(solution)/shard_map/ppermute | solution.py:28
Sparse Core Ops, SparseCore 0:
  29.8 103.5 all-gather.1
where the time goes:
time: 276 us; the launch traced here: 275 us
  waiting for transfers between devices  177 us (64%)
  between operations  31.7 us (11%)
  blocking collectives  20.7 us (8%)
  local copies, waits for them, and re-layouts  16 us (6%)
  matrix products  14.2 us (5%)
  starting transfers between devices  11.4 us (4%)
  other arithmetic  4.01 us (1%)
    all_gather x1, waiting for transfers between devices, shards(): half_a = lax.all_gather(spread_a, 'colx', axis=0, tiled=True)  104 us
    ppermute x4, waiting for transfers between devices, ring_gather(): go_right = lax.ppermute(go_right, axis, right)  58.8 us
    all_to_all x1, blocking collectives, shards(): lax.all_to_all(factors.reshape(local_aux, nocc, n_row, rows_a), 'row', sp...  20.7 us
    all_to_all x1, waiting for transfers between devices, shards(): lax.all_to_all(factors.reshape(local_aux, nocc, n_col, cols_b), ('colx',...  14.6 us
    dot_general x1, matrix products, shards(): jnp.einsum(contract, other_a.reshape(n_colx, n_row, local_aux, nocc, rows...  7.69 us
    dot_general x1, matrix products, shards(): jnp.einsum(contract, half_a.reshape(n_colx, n_row, local_aux, nocc, rows_...  6.54 us
    ppermute x4, starting transfers between devices, ring_gather(): go_right = lax.ppermute(go_right, axis, right)  6.08 us
  transfers between devices with their start and end apart: 10, of which 5 were waited for; matrix products, arithmetic and copies ran while one was open for 5% of the time, Pallas kernels for 0%

commit v1 on v0

--- a/solution.py
+++ b/solution.py
@@ -48,7 +48,9 @@
         concat_axis=0,
         tiled=True,
     ).reshape(n_row * local_aux, nocc, rows_a)
-    half_a = lax.all_gather(spread_a, "colx", axis=0, tiled=True)
+    half_a = jnp.concatenate(
+        lax.all_to_all(jnp.stack([spread_a] * lax.axis_size("colx")), "colx", 0, 0), axis=0
+    )
     other_a = lax.ppermute(half_a, "core", [(k, (k + 1) % n_core) for k in range(n_core)])
     spread_b = lax.all_to_all(
         factors.reshape(local_aux, nocc, n_col, cols_b),

time: 276 us -> 259 us (0.938)
  waiting for transfers between devices: 177 us -> 73.7 us
  blocking collectives: 20.7 us -> 117 us
  between operations: 31.7 us -> 18.1 us
  local copies, waits for them, and re-layouts: 16 us -> 22.6 us
    all_gather x1 -> x0, waiting for transfers between devices: 104 us -> none  [shards(): half_a = lax.all_gather(spread_a, 'colx', axis=0, tiled=True)]
    all_to_all x0 -> x1, blocking collectives: none -> 96 us  [shards(): lax.all_to_all(jnp.stack([spread_a] * lax.axis_size('colx')), 'colx', 0, 0)]
    all_to_all x0 -> x1, local copies, waits for them, and re-layouts: none -> 3.89 us  [shards(): lax.all_to_all(jnp.stack([spread_a] * lax.axis_size('colx')), 'colx', 0, 0)]
  transfers between devices with their start and end apart: 10 -> 9, of which waited for: 5 -> 4; matrix products, arithmetic and copies ran while one was open for 5% -> 6% of each run, Pallas kernels for 0% -> 0%
where the time goes in v1:
time: 259 us; the launch traced here: 258 us
  blocking collectives  117 us (45%)
  waiting for transfers between devices  73.7 us (28%)
  local copies, waits for them, and re-layouts  22.6 us (9%)
  between operations  18.1 us (7%)
  matrix products  12.2 us (5%)
  starting transfers between devices  11.2 us (4%)
  other arithmetic  3.87 us (1%)
    all_to_all x1, blocking collectives, shards(): lax.all_to_all(jnp.stack([spread_a] * lax.axis_size('colx')), 'colx', 0, 0)  96 us
    ppermute x4, waiting for transfers between devices, ring_gather(): go_right = lax.ppermute(go_right, axis, right)  58.9 us
    all_to_all x1, blocking collectives, shards(): lax.all_to_all(factors.reshape(local_aux, nocc, n_row, rows_a), 'row', sp...  20.7 us
    all_to_all x1, waiting for transfers between devices, shards(): lax.all_to_all(factors.reshape(local_aux, nocc, n_col, cols_b), ('colx',...  14.8 us
    dot_general x1, matrix products, shards(): jnp.einsum(contract, other_a.reshape(n_colx, n_row, local_aux, nocc, rows...  7.83 us
    ppermute x4, starting transfers between devices, ring_gather(): go_right = lax.ppermute(go_right, axis, right)  5.44 us
  transfers between devices with their start and end apart: 9, of which 4 were waited for; matrix products, arithmetic and copies ran while one was open for 6% of the time, Pallas kernels for 0%

profile of v1, /device:TPU:0, one launch (start us, length us, event | category | flops | bytes accessed | tf_op | source)
XLA Modules:
  0.0 258.4 jit_solution(5902699984389085488)
XLA Ops:
  0.0 1.3 copy.74
  1.3 20.7 %all_to_all.35 = bf16[80,3,8,256]{3,0,1,2:T(8,128)(2,1)S(1)} all-to-all(bf16[80,3,8,256]{3,0,1,2:T(8,128)(2,1)S(1)} %bitcast.123), channel_id=1, replica_groups=mesh['row'=8,'colx'=8,'core'=2] {'row'}, dimensions={2} | all-to-all | bytes 1966080 | tf_op jit(solution)/shard_map/all_to_all | solution.py:44
  22.1 0.8 stack.3
  22.9 96.0 %all_to_all.36 = bf16[8,640,3,256]{3,1,2,0:T(8,128)(2,1)S(1)} all-to-all(bf16[8,640,3,256]{3,1,2,0:T(8,128)(2,1)S(1)} %stack.3), channel_id=1, replica_groups=mesh['row'=8,'colx'=8,'core'=2] {'colx'}, dimensions={0} | all-to-all | bytes 15728640 | tf_op jit(solution)/shard_map/all_to_all | solution.py:52
  119.0 3.9 %copy.31 = bf16[8,640,3,256]{3,1,0,2:T(8,128)(2,1)} copy(bf16[8,640,3,256]{3,1,2,0:T(8,128)(2,1)S(1)} %all_to_all.36) | data formatting | bytes 15728640 | tf_op jit(solution)/shard_map/all_to_all | solution.py:52
  122.9 1.5 copy-done.3
  124.4 1.1 copy_bitcast_fusion.1
  125.5 3.6 %all-to-all-start = ((bf16[80,3,16,128]{3,0,1,2:T(8,128)(2,1)}), bf16[80,3,16,128]{3,0,1,2:T(8,128)(2,1)S(1)}, u32[]{:S(2)}, u32[]{:S(2)}) async-start(bf16[80,3,16,128]{3,0,1,2:T(8,128)(2,1)} %copy_bitcast_fusion.1), calls=%async_computation | async-start | bytes 1966080 | tf_op jit(solution)/shard_map/all_to_all | solution.py:55
  129.8 1.8 fusion.30
  131.6 14.8 %all-to-all-done = bf16[80,3,16,128]{3,0,1,2:T(8,128)(2,1)S(1)} async-done(((bf16[80,3,16,128]{3,0,1,2:T(8,128)(2,1)}), bf16[80,3,16,128]{3,0,1,2:T(8,128)(2,1)S(1)}, u32[]{:S(2)}, u32[]{:S(2)}) %all-to-all-start) | async-done | bytes 983072 | tf_op jit(solution)/shard_map/all_to_all | solution.py:55
  146.5 1.4 collective-permute-start
  147.9 0.7 collective-permute-start.1
  153.8 0.7 fusion.33
  163.3 0.8 dynamic_slice.48
  164.0 0.8 dynamic_slice.47
  164.8 0.7 gather_fusion.1
  165.5 0.7 gather_fusion.2
  171.3 1.7 broadcast_in_dim.51
  173.2 1.4 collective-permute-start.2
  174.6 0.7 collective-permute-start.3
  175.6 20.2 %collective-permute-done.2 = bf16[1280,3,128]{2,0,1:T(8,128)(2,1)S(1)} collective-permute-done((bf16[1280,3,128]{2,0,1:T(8,128)(2,1)S(1)}, bf16[1280,3,128]{2,0,1:T(8,128)(2,1)S(1)}, u32[]{:S(2)}, u32[]{:S(2)}) %collective-permute-start.2) | collective-permute-done | bytes 983072 | tf_op jit(solution)/shard_map/ppermute | solution.py:28
  195.7 1.3 collective-permute-start.4
  197.0 0.7 collective-permute-start.5
  198.0 19.6 %collective-permute-done.4 = bf16[1280,3,128]{2,0,1:T(8,128)(2,1)S(1)} collective-permute-done((bf16[1280,3,128]{2,0,1:T(8,128)(2,1)S(1)}, bf16[1280,3,128]{2,0,1:T(8,128)(2,1)S(1)}, u32[]{:S(2)}, u32[]{:S(2)}) %collective-permute-start.4) | collective-permute-done | bytes 983072 | tf_op jit(solution)/shard_map/ppermute | solution.py:28
  217.6 1.3 collective-permute-start.6
  219.2 19.2 %collective-permute-done.6 = bf16[1280,3,128]{2,0,1:T(8,128)(2,1)S(1)} collective-permute-done((bf16[1280,3,128]{2,0,1:T(8,128)(2,1)S(1)}, bf16[1280,3,128]{2,0,1:T(8,128)(2,1)S(1)}, u32[]{:S(2)}, u32[]{:S(2)}) %collective-permute-start.6) | collective-permute-done | bytes 983072 | tf_op jit(solution)/shard_map/ppermute | solution.py:28
  238.5 3.4 %constant_dynamic-slice_fusion.1 = (bf16[8,8,1,80,3,128]{5,3,2,1,4,0:T(8,128)(2,1)S(1)}, bf16[8,8,1,80,3,128]{5,3,2,1,4,0:T(8,128)(2,1)}) fusion(bf16[8,8,2,80,3,128]{5,3,2,1,4,0:T(8,128)(2,1)S(1)} %bitcast.115, s32[]{:T(128)S(6)} %select_n.160, s32[]{:T(128)S(6)} %select_n.162), kind=kLoop, calls=%fused_computation.40 | loop fusion | bytes 15728648 | tf_op jit(solution)/shard_map/jit(dynamic_index_in_dim)/dynamic_slice | solution.py:69
  241.9 7.8 %fusion.15 = f32[3,128,3,256]{3,1,2,0:T(8,128)S(1)} fusion(bf16[8,8,80,3,256]{4,2,1,0,3:T(8,128)(2,1)} %bitcast.43, bf16[8,8,1,80,3,128]{5,3,2,1,4,0:T(8,128)(2,1)} %get-tuple-element.8), kind=kOutput, calls=%fused_computation.16 | convolution fusion | flops 3019898880 | bytes 12976128 | tf_op jit(solution)/shard_map/xrpia,rxpjb->ijab/dot_general | solution.py:71
  249.8 4.3 %fusion.25 = f32[3,3,256,128]{2,3,0,1:T(8,128)} fusion(f32[3,128,3,256]{3,1,2,0:T(8,128)S(1)} %fusion.15, bf16[8,8,80,3,256]{4,2,1,3,0:T(8,128)(2,1)S(1)} %bitcast.114, bf16[8,8,1,80,3,128]{5,3,2,1,4,0:T(8,128)(2,1)S(1)} %get-tuple-element.7), kind=kOutput, calls=%fused_computation.18 | convolution fusion | flops 3020193792 | bytes 14155776 | tf_op jit(solution)/shard_map/xrpia,rxpjb->ijab/dot_general | solution.py:66
  254.1 1.6 copy.33
  255.8 0.7 gather_fusion
  256.4 1.9 add_divide_fusion
  (47 shorter events, 3.3 us)
Async XLA Ops:
  0.0 164.8 %copy-start = (f32[300]{0:T(512)S(1)}, f32[300]{0:T(512)}, u32[]{:S(2)}) copy-start(f32[300]{0:T(512)} %param.10) | copy-start | bytes 3604
  119.0 5.4 %copy-start.3 = (bf16[8,640,3,256]{3,1,2,0:T(8,128)(2,1)}, bf16[8,640,3,256]{3,1,2,0:T(8,128)(2,1)S(1)}, u32[]{:S(2)}) copy-start(bf16[8,640,3,256]{3,1,2,0:T(8,128)(2,1)S(1)} %all_to_all.36) | copy-start | bytes 23592964
  119.0 5.4 %copy-start.4 = (bf16[80,3,2048]{2,0,1:T(8,128)(2,1)S(1)}, bf16[80,3,2048]{2,0,1:T(8,128)(2,1)}, u32[]{:S(2)}) copy-start(bf16[80,3,2048]{2,0,1:T(8,128)(2,1)} %param.9) | copy-start | bytes 2949124
  119.0 10.2 %copy-start.6 = (s32[3]{0:T(128)S(1)}, s32[3]{0:T(128)}, u32[]{:S(2)}) copy-start(s32[3]{0:T(128)} %param.12) | copy-start | bytes 40
  119.0 10.8 %copy-start.8 = (s32[16]{0:T(128)S(1)}, s32[16]{0:T(128)}, u32[]{:S(2)}) copy-start(s32[16]{0:T(128)} %param.14) | copy-start | bytes 196
  119.0 10.8 %copy-start.7 = (s32[16,2]{0,1:T(2,128)S(1)}, s32[16,2]{0,1:T(2,128)}, u32[]{:S(2)}) copy-start(s32[16,2]{0,1:T(2,128)} %param.13) | copy-start | bytes 388
  119.0 29.6 %copy-start.5 = (s32[8]{0:T(128)S(1)}, s32[8]{0:T(128)}, u32[]{:S(2)}) copy-start(s32[8]{0:T(128)} %constant.138.clone) | copy-start | bytes 100
  119.0 51.5 %copy-start.2 = (f32[4]{0:T(128)S(1)}, f32[4]{0:T(128)}, u32[]{:S(2)}) copy-start(f32[4]{0:T(128)} %param.15) | copy-start | bytes 52
  124.4 117.5 %collective-permute-start.7 = (bf16[5120,3,256]{2,0,1:T(8,128)(2,1)}, bf16[5120,3,256]{2,0,1:T(8,128)(2,1)}, u32[]{:S(2)}, u32[]{:S(2)}) collective-permute-start(bf16[5120,3,256]{2,0,1:T(8,128)(2,1)} %bitcast.117), channel_id=1, source_target_pairs={{0,1},{1,0},{2,3},{3,2},{4,5},{5,4},{6,7},{7,6},{8,9},{9,8},{10,11... | collective-permute-start | bytes 23592968 | tf_op jit(solution)/shard_map/ppermute | solution.py:54
  125.5 20.9 %all-to-all-start = ((bf16[80,3,16,128]{3,0,1,2:T(8,128)(2,1)}), bf16[80,3,16,128]{3,0,1,2:T(8,128)(2,1)S(1)}, u32[]{:S(2)}, u32[]{:S(2)}) async-start(bf16[80,3,16,128]{3,0,1,2:T(8,128)(2,1)} %copy_bitcast_fusion.1), calls=%async_computation | async-start | bytes 1966080 | tf_op jit(solution)/shard_map/all_to_all | solution.py:55
  146.5 26.7 %collective-permute-start = (bf16[1280,3,128]{2,0,1:T(8,128)(2,1)S(1)}, bf16[1280,3,128]{2,0,1:T(8,128)(2,1)S(1)}, u32[]{:S(2)}, u32[]{:S(2)}) collective-permute-start(bf16[1280,3,128]{2,0,1:T(8,128)(2,1)S(1)} %bitcast.119), channel_id=1, source_target_pairs={{0,16},{16,32},{32,48},{48,112},{112,96},{96,80},{80,64},{64,0},{1... | collective-permute-start | bytes 2949128 | tf_op jit(solution)/shard_map/ppermute | solution.py:28
  147.9 26.7 %collective-permute-start.1 = (bf16[1280,3,128]{2,0,1:T(8,128)(2,1)S(1)}, bf16[1280,3,128]{2,0,1:T(8,128)(2,1)S(1)}, u32[]{:S(2)}, u32[]{:S(2)}) collective-permute-start(bf16[1280,3,128]{2,0,1:T(8,128)(2,1)S(1)} %bitcast.120), channel_id=1, source_target_pairs={{0,64},{16,0},{32,16},{48,32},{112,48},{96,112},{80,96},{64,80},{1... | collective-permute-start | bytes 2949128 | tf_op jit(solution)/shard_map/ppermute | solution.py:31
  173.2 22.5 %collective-permute-start.2 = (bf16[1280,3,128]{2,0,1:T(8,128)(2,1)S(1)}, bf16[1280,3,128]{2,0,1:T(8,128)(2,1)S(1)}, u32[]{:S(2)}, u32[]{:S(2)}) collective-permute-start(bf16[1280,3,128]{2,0,1:T(8,128)(2,1)S(1)} %collective-permute-done), channel_id=1, source_target_pairs={{0,16},{16,32},{32,48},{48,112},{112,96},{96,80},{80,64},{64,0},{1... | collective-permute-start | bytes 2949128 | tf_op jit(solution)/shard_map/ppermute | solution.py:28
  174.6 22.4 %collective-permute-start.3 = (bf16[1280,3,128]{2,0,1:T(8,128)(2,1)S(1)}, bf16[1280,3,128]{2,0,1:T(8,128)(2,1)S(1)}, u32[]{:S(2)}, u32[]{:S(2)}) collective-permute-start(bf16[1280,3,128]{2,0,1:T(8,128)(2,1)S(1)} %collective-permute-done.1), channel_id=1, source_target_pairs={{0,64},{16,0},{32,16},{48,32},{112,48},{96,112},{80,96},{64,80},{1... | collective-permute-start | bytes 2949128 | tf_op jit(solution)/shard_map/ppermute | solution.py:31
  195.7 21.9 %collective-permute-start.4 = (bf16[1280,3,128]{2,0,1:T(8,128)(2,1)S(1)}, bf16[1280,3,128]{2,0,1:T(8,128)(2,1)S(1)}, u32[]{:S(2)}, u32[]{:S(2)}) collective-permute-start(bf16[1280,3,128]{2,0,1:T(8,128)(2,1)S(1)} %collective-permute-done.2), channel_id=1, source_target_pairs={{0,16},{16,32},{32,48},{48,112},{112,96},{96,80},{80,64},{64,0},{1... | collective-permute-start | bytes 2949128 | tf_op jit(solution)/shard_map/ppermute | solution.py:28
  197.0 22.1 %collective-permute-start.5 = (bf16[1280,3,128]{2,0,1:T(8,128)(2,1)S(1)}, bf16[1280,3,128]{2,0,1:T(8,128)(2,1)S(1)}, u32[]{:S(2)}, u32[]{:S(2)}) collective-permute-start(bf16[1280,3,128]{2,0,1:T(8,128)(2,1)S(1)} %collective-permute-done.3), channel_id=1, source_target_pairs={{0,64},{16,0},{32,16},{48,32},{112,48},{96,112},{80,96},{64,80},{1... | collective-permute-start | bytes 2949128 | tf_op jit(solution)/shard_map/ppermute | solution.py:31
  217.6 20.8 %collective-permute-start.6 = (bf16[1280,3,128]{2,0,1:T(8,128)(2,1)S(1)}, bf16[1280,3,128]{2,0,1:T(8,128)(2,1)S(1)}, u32[]{:S(2)}, u32[]{:S(2)}) collective-permute-start(bf16[1280,3,128]{2,0,1:T(8,128)(2,1)S(1)} %collective-permute-done.4), channel_id=1, source_target_pairs={{0,16},{16,32},{32,48},{48,112},{112,96},{96,80},{80,64},{64,0},{1... | collective-permute-start | bytes 2949128 | tf_op jit(solution)/shard_map/ppermute | solution.py:28
  238.5 11.2 %slice-start = ((s8[7864320]{0:T(1024)(128)(4,1)}), s8[3670016]{0:T(1024)(128)(4,1)S(1)}, s32[]{:S(2)}) async-start(s8[7864320]{0:T(1024)(128)(4,1)} %bitcast.112), calls=%async_computation.3 | async-start | bytes 7340032
  241.9 7.8 %slice-start.1 = ((s8[7864320]{0:T(1024)(128)(4,1)}), s8[4194304]{0:T(1024)(128)(4,1)S(1)}, s32[]{:S(2)}) async-start(s8[7864320]{0:T(1024)(128)(4,1)} %bitcast.112), calls=%async_computation.4 | async-start | bytes 8388608
  249.8 8.6 %copy-start.1 = (f32[300]{0:T(512)S(1)}, f32[300]{0:T(512)}, u32[]{:S(2)}) copy-start(f32[300]{0:T(512)} %param.10) | copy-start | bytes 3604
